TPU v7x, 512 devices: a whole 4x8x8 slice. The times are simulated.
512 devices in a mesh: rep: 8 (over y_lo, core), seq: 2 (over y_hi), tp: 32 (over x, z).
Axes of the slice: x: 4, y: 8 (y_hi: 2, y_lo: 4; y = y_hi * 4 + y_lo), z: 8, core: 2. Of those that a mesh axis runs over, the one named last changes fastest.
Arguments:
- hidden: bfloat16 [3072, 8192], P('rep', ('seq', 'tp')), may hold values from -100 to 100
- gain: float32 [8192], replicated, may hold values from 0.1 to 1.9
- w_query: bfloat16 [8192, 8192], P('seq', 'tp'), may hold values from -1 to 1
- w_keyval: bfloat16 [2, 4096, 2048], P(None, 'tp'), may hold values from -1 to 1
- lengths: int32 [8, 2], replicated, may hold values from 128 to 192, as said below
- routes: int32 [8, 2], replicated, may hold values from 0 to 7, as said below
Outputs:
- attended: bfloat16 [3072, 8192], P(('rep', 'seq'), 'tp')
Inputs may be any that keep to these rules, and one draw needn't show every extreme that they name: `routes`: for each j, the responses j of the 8 rollout groups go to 8 different replicas, so each replica receives exactly 2 responses. `lengths`: the responses that one rollout group sends to one replica hold at most 192 tokens together, and in every draw some group sends exactly 192 tokens to one replica.
All inputs are finite; a program needn't handle non-finite values.
Results may differ from a plain program's by a relative error of at most 0.0076.
Values may be sent and summed in bfloat16 or wider, within the bound.
No kernel may reach another device: no remote copies, remote signals or barrier semaphores. Data moves between devices by JAX's collectives and lax.ppermute only.
A program may use at most 64 MiB of HBM per device.

v0:
```python
import math
import jax
import jax.numpy as jnp
from jax import lax
from jax.sharding import PartitionSpec as P

D = 8192
QH = 64
KVH = 8
HD = 128
RESP = 2
LMAX = 192
BUFFER = 384
ROPE_BASE = 500000.0
NORM_EPS = 1e-05
MASK_FILL = -1e30


def response_tables(lengths, routes):
    flat_len = lengths.reshape(-1)
    flat_route = routes.reshape(-1)
    response_ids = jnp.arange(flat_len.shape[0], dtype=jnp.int32)
    group_of = response_ids // RESP
    same_route = flat_route[:, None] == flat_route[None, :]
    same_group = group_of[:, None] == group_of[None, :]
    earlier = response_ids[None, :] < response_ids[:, None]
    dest_off = jnp.sum(jnp.where(same_route & earlier, flat_len[None, :], 0), axis=1)
    pair_off = jnp.sum(jnp.where(same_route & same_group & earlier, flat_len[None, :], 0), axis=1)
    src_start = jnp.sum(jnp.where(same_group & earlier, flat_len[None, :], 0), axis=1)
    return (flat_len, flat_route, group_of, dest_off, pair_off, src_start)


def locate(positions, replica, tables):
    flat_len, flat_route, group_of, dest_off, pair_off, src_start = tables
    response_ids = jnp.arange(flat_len.shape[0], dtype=jnp.int32)
    position_col = positions[:, None]
    inside = (
        (flat_route[None, :] == replica)
        & (dest_off[None, :] <= position_col)
        & (position_col < dest_off[None, :] + flat_len[None, :])
    )
    inside_int = inside.astype(jnp.int32)
    segment = jnp.sum(inside_int * (response_ids[None, :] + 1), axis=1) - 1
    seg_start = jnp.sum(inside_int * dest_off[None, :], axis=1)
    source_group = jnp.sum(inside_int * group_of[None, :], axis=1)
    pair_first = jnp.sum(inside_int * (dest_off - pair_off)[None, :], axis=1)
    source = jnp.sum(inside_int * src_start[None, :], axis=1)
    within = jnp.where(segment >= 0, positions - seg_start, 0)
    return (segment, within, source_group, pair_first, source)


def rotary(values_in, within):
    head_dim = values_in.shape[-1]
    half_dim = head_dim // 2
    freq_index = jnp.arange(half_dim, dtype=jnp.float32)
    inverse = jnp.power(ROPE_BASE, -2.0 * freq_index / head_dim)
    angles = within.astype(jnp.float32)[:, None] * inverse[None, :]
    cosine = jnp.cos(angles)[:, None, :]
    sine_part = jnp.sin(angles)[:, None, :]
    lower_half = values_in[..., :half_dim]
    upper_half = values_in[..., half_dim:]
    return jnp.concatenate(
        [
            lower_half * cosine - upper_half * sine_part,
            upper_half * cosine + lower_half * sine_part,
        ],
        axis=-1,
    )


def fill_rows(table, indices, present):
    taken = jnp.take(table, indices.reshape(-1), axis=0)
    return jnp.where(present.reshape(-1)[:, None], taken, jnp.zeros((), table.dtype))


def local(hidden, gain, w_query, w_keyval, lengths, routes):
    rep_count = lax.axis_size("rep")
    seq_count = lax.axis_size("seq")
    replica = lax.axis_index("rep")
    seq_index = lax.axis_index("seq")
    column = lax.axis_index("tp")
    feature_cols = hidden.shape[1]
    local_rows = BUFFER // seq_count
    capacity = (RESP + rep_count - 1) // rep_count * LMAX
    head_count = w_query.shape[1] // HD
    tables = response_tables(lengths, routes)
    flat_len, flat_route, group_of, dest_off, pair_off, src_start = tables
    my_len = lax.dynamic_slice_in_dim(flat_len, replica * RESP, RESP)
    my_route = lax.dynamic_slice_in_dim(flat_route, replica * RESP, RESP)
    my_pair = lax.dynamic_slice_in_dim(pair_off, replica * RESP, RESP)
    my_start = lax.dynamic_slice_in_dim(src_start, replica * RESP, RESP)
    slot_ids = jnp.arange(capacity, dtype=jnp.int32)
    targets = jnp.arange(rep_count, dtype=jnp.int32)
    block_off = jnp.broadcast_to(slot_ids[None, :], (rep_count, capacity))
    offsets = block_off[:, :, None]
    inside = (
        (my_route[None, None, :] == targets[:, None, None])
        & (my_pair[None, None, :] <= offsets)
        & (offsets < (my_pair + my_len)[None, None, :])
    )
    inside_int = inside.astype(jnp.int32)
    src_rows = jnp.sum(
        inside_int * (my_start[None, None, :] + offsets - my_pair[None, None, :]), axis=2
    )
    src_rows, present = (src_rows, jnp.any(inside, axis=2))
    outgoing = fill_rows(hidden, src_rows, present)
    incoming = lax.all_to_all(outgoing, "rep", split_axis=0, concat_axis=0, tiled=True)
    all_pos = jnp.arange(BUFFER, dtype=jnp.int32)
    segment, within, source_group, pair_first, source = locate(all_pos, replica, tables)
    gathered_idx = jnp.where(segment >= 0, source_group * capacity + all_pos - pair_first, 0)
    assembled = fill_rows(incoming, gathered_idx, segment >= 0)
    local_x = lax.all_to_all(
        assembled.reshape(BUFFER, 1, feature_cols), "seq", split_axis=0, concat_axis=1, tiled=True
    )
    query_pos = seq_index * local_rows + jnp.arange(local_rows, dtype=jnp.int32)
    query_info = locate(query_pos, replica, tables)
    query_seg = query_info[0]
    query_within = query_info[1]
    query_valid = query_seg >= 0
    gain_halves = gain.reshape(seq_count, D // seq_count)
    gain_local = lax.dynamic_slice_in_dim(gain_halves, column * feature_cols, feature_cols, 1)
    kv_head = column * head_count // (QH // KVH)
    query_weights = lax.all_gather(
        w_query.reshape(1, w_query.shape[0], w_query.shape[1]), "seq", axis=0, tiled=True
    )
    feature_piece = lax.all_gather(local_x, "tp", axis=2, tiled=True)
    scaled_piece = (feature_piece.astype(jnp.float32) * gain_halves[None]).astype(jnp.bfloat16)
    query_acc = jnp.einsum(
        "rsn,snf->rf", scaled_piece, query_weights, preferred_element_type=jnp.float32
    )
    squares = jnp.sum(jnp.square(feature_piece.astype(jnp.float32)), axis=(1, 2))
    inverse_rms = lax.rsqrt(squares / D + NORM_EPS)
    queries = rotary(
        inverse_rms[:, None, None] * query_acc.reshape(local_rows, head_count, HD), query_within
    ).astype(jnp.bfloat16)
    scaled_local = (local_x.astype(jnp.float32) * gain_local[None]).astype(jnp.bfloat16)
    kv_partial = jnp.einsum(
        "rsw,swc->rc", scaled_local, w_keyval, preferred_element_type=jnp.float32
    )
    kv_total = lax.psum(kv_partial, "tp")
    head_block = lax.dynamic_slice_in_dim(kv_total, kv_head * 2 * HD, 2 * HD, 1)
    keys = rotary(inverse_rms[:, None, None] * head_block[:, None, :HD], query_within)[:, 0].astype(
        jnp.bfloat16
    )
    values = (inverse_rms[:, None] * head_block[:, HD:]).astype(jnp.bfloat16)
    score_scale = 1.0 / math.sqrt(HD)
    running = jnp.full((local_rows, head_count), MASK_FILL, jnp.float32)
    key_part = lax.all_gather(keys, "seq", axis=0, tiled=True)
    value_part = lax.all_gather(values, "seq", axis=0, tiled=True)
    key_count = key_part.shape[0]
    key_pos = jnp.arange(key_count, dtype=jnp.int32)
    key_seg = locate(key_pos, replica, tables)[0]
    allowed = (key_seg[None, :] == query_seg[:, None]) & query_valid[:, None] & (
        key_pos[None, :] <= query_pos[:, None]
    ) | (key_pos[None, :] == query_pos[:, None])
    scores = (
        jnp.einsum("rhd,kd->rhk", queries, key_part, preferred_element_type=jnp.float32)
        * score_scale
    )
    scores = jnp.where(allowed[:, None, :], scores, MASK_FILL)
    new_max = jnp.maximum(running, jnp.max(scores, axis=2))
    prob_terms = jnp.where(allowed[:, None, :], jnp.exp(scores - new_max[:, :, None]), 0.0)
    totals = jnp.sum(prob_terms, axis=2)
    accum = jnp.einsum(
        "rhk,kd->rhd",
        prob_terms.astype(jnp.bfloat16),
        value_part,
        preferred_element_type=jnp.float32,
    )
    attended = (
        (accum / totals[:, :, None]).reshape(local_rows, head_count * HD).astype(jnp.bfloat16)
    )
    return jnp.where(query_valid[:, None], attended, jnp.zeros((), jnp.bfloat16))


def solution(mesh):
    in_specs = (P("rep", ("seq", "tp")), P(), P("seq", "tp"), P(None, "tp", None), P(), P())
    out_specs = P(("rep", "seq"), "tp")
    return jax.shard_map(local, mesh=mesh, in_specs=in_specs, out_specs=out_specs, check_vma=False)
```

profile of v0, /device:TPU:16, one launch (start us, length us, event | category | flops | bytes accessed | tf_op | source)
XLA Modules:
  0.0 440.9 jit_solution(4229495986316716021)
XLA Ops:
  6.5 0.8 copy.25
  7.5 0.8 copy.24
  8.4 0.2 select_reduce_fusion.7
  9.1 3.5 gather_fusion
  12.7 1.3 select_select_fusion
  14.0 9.1 %all-to-all-start = ((bf16[8,192,128]{2,1,0:T(8,128)(2,1)}), bf16[8,192,128]{2,1,0:T(8,128)(2,1)S(1)}, u32[]{:S(2)}, u32[]{:S(2)}) async-start(bf16[8,192,128]{2,1,0:T(8,128)(2,1)} %select_select_fusion), calls=%async_computation | async-start | bytes 786432 | tf_op jit(solution)/shard_map/all_to_all | solution.py:107
  23.1 0.1 select_reduce_fusion.1
  23.3 9.1 %all-to-all-done = bf16[8,192,128]{2,1,0:T(8,128)(2,1)S(1)} async-done(((bf16[8,192,128]{2,1,0:T(8,128)(2,1)}), bf16[8,192,128]{2,1,0:T(8,128)(2,1)S(1)}, u32[]{:S(2)}, u32[]{:S(2)}) %all-to-all-start) | async-done | bytes 393248 | tf_op jit(solution)/shard_map/all_to_all | solution.py:107
  32.4 1.4 gather_fusion.1
  33.8 0.2 fusion.37
  34.0 0.5 broadcast.494
  34.5 0.7 reduce.4
  35.2 10.6 %all_to_all.27 = bf16[2,2,12288]{2,1,0:T(2,128)(2,1)S(1)} all-to-all(bf16[2,2,12288]{2,1,0:T(2,128)(2,1)S(1)} %reshape.481), channel_id=1, replica_groups=mesh['rep'=8,'seq'=2,'tp'=32] {'seq'}, dimensions={0} | all-to-all | bytes 196608 | tf_op jit(solution)/shard_map/all_to_all | solution.py:112
  45.9 0.7 copy.29
  46.6 0.7 all-gather.8.cloned.1.call-update
  47.6 0.2 fusion.18
  47.8 2.5 convolution_bitcast_fusion
  50.3 0.4 multiply_cosine_fusion.1
  50.7 82.6 %all-gather.6.cloned.1.call-done = bf16[192,2,1,4096]{3,0,1,2:T(8,128)(2,1)} async-done(((bf16[192,2,1,128]{3,0,1,2:T(8,128)(2,1)}), bf16[192,2,1,4096]{3,0,1,2:T(8,128)(2,1)}) %all-gather.6.cloned.1.call-update) | async-done | bytes 3145744 | tf_op jit(solution)/shard_map/all_gather | solution.py:126
  133.3 2.6 fusion
  135.9 111.5 %all-gather.8.cloned.1.call-done = bf16[8192,256]{1,0:T(8,128)(2,1)} async-done(((bf16[4096,256]{1,0:T(8,128)(2,1)}), bf16[8192,256]{1,0:T(8,128)(2,1)}) %all-gather.8.cloned.1.call-update) | async-done | bytes 4194320 | tf_op jit(solution)/shard_map/all_gather | solution.py:123
  247.4 4.1 fusion.7
  251.7 161.3 %all-reduce.2.cloned.1.call-done = f32[192,2048]{1,0:T(8,128)} async-done(((f32[192,2048]{1,0:T(8,128)}), f32[192,2048]{1,0:T(8,128)}) %all-reduce.2.cloned.1.call-update) | async-done | bytes 1572880 | tf_op jit(solution)/shard_map/psum | solution.py:140
  412.9 1.0 fusion.30
  413.9 0.5 fusion.26
  414.5 9.2 %all-gather.2 = bf16[384,1,128]{2,0,1:T(8,128)(2,1)S(1)} all-gather(bf16[192,1,128]{2,0,1:T(8,128)(2,1)S(1)} %pad_maximum_fusion), channel_id=4, replica_groups=mesh['rep'=8,'seq'=2,'tp'=32] {'seq'}, dimensions={0}, use_global_device_ids=true | all-gather | bytes 147456 | tf_op jit(solution)/shard_map/all_gather | solution.py:148
  423.7 0.1 subtract_convert_fusion
  423.9 0.4 fusion.50
  424.3 8.7 %all_gather.15 = bf16[384,128]{1,0:T(8,128)(2,1)S(1)} all-gather(bf16[192,128]{1,0:T(8,128)(2,1)S(1)} %get-tuple-element.19), channel_id=1, replica_groups=mesh['rep'=8,'seq'=2,'tp'=32] {'seq'}, dimensions={0}, use_global_device_ids=true | all-gather | bytes 147456 | tf_op jit(solution)/shard_map/all_gather | solution.py:149
  433.0 0.3 fusion.12
  433.3 0.3 fusion.11
  433.7 0.7 bitcast_select_fusion
  (41 shorter events, 1.4 us)
Async XLA Ops:
  6.5 41.2 %copy-start = (bf16[2,128,2048]{2,1,0:T(8,128)(2,1)S(1)}, bf16[2,128,2048]{2,1,0:T(8,128)(2,1)}, u32[]{:S(2)}) copy-start(bf16[2,128,2048]{2,1,0:T(8,128)(2,1)} %param.9) | copy-start | bytes 3145732
  12.7 34.7 %copy-start.1 = (f32[8192]{0:T(1024)S(1)}, f32[8192]{0:T(1024)}, u32[]{:S(2)}) copy-start(f32[8192]{0:T(1024)} %param.7) | copy-start | bytes 98308
  14.0 18.4 %all-to-all-start = ((bf16[8,192,128]{2,1,0:T(8,128)(2,1)}), bf16[8,192,128]{2,1,0:T(8,128)(2,1)S(1)}, u32[]{:S(2)}, u32[]{:S(2)}) async-start(bf16[8,192,128]{2,1,0:T(8,128)(2,1)} %select_select_fusion), calls=%async_computation | async-start | bytes 786432 | tf_op jit(solution)/shard_map/all_to_all | solution.py:107
  23.1 110.2 %all-gather.6.cloned.1.call-start = ((), (), s32[]{:S(2)}) async-start(), calls=%async_computation.3 | async-start | bytes 3244032 | tf_op jit(solution)/shard_map/all_gather | solution.py:126
  46.6 200.9 %all-gather.8.cloned.1.call-start = ((), (), s32[]{:S(2)}) async-start(), calls=%async_computation.4 | async-start | bytes 6291456 | tf_op jit(solution)/shard_map/all_gather | solution.py:123
  47.3 365.6 %all-reduce.2.cloned.1.call-start = ((), (), s32[]{:S(2)}) async-start(), calls=%async_computation.2 | async-start | bytes 3145728 | tf_op jit(solution)/shard_map/psum | solution.py:140
Sparse Core Ops, SparseCore 0:
  46.7 86.6 all-gather.5
  135.4 111.9 all-gather.7
  250.8 162.0 all-reduce.1
where the time goes:
time: 441 us
  waiting for transfers between devices  365 us (83%)
  blocking collectives  28.5 us (6%)
  between operations  13.4 us (3%)
  starting transfers between devices  9.17 us (2%)
  other arithmetic  9.02 us (2%)
  local copies, waits for them, and re-layouts  8.3 us (2%)
  matrix products  7.34 us (2%)
    psum x1, waiting for transfers between devices, local(): kv_total = lax.psum(kv_partial, 'tp')  161 us
    all_gather x1, waiting for transfers between devices, local(): lax.all_gather(w_query.reshape(1, w_query.shape[0], w_query.shape[1]), 's...  111 us
    all_gather x1, waiting for transfers between devices, local(): feature_piece = lax.all_gather(local_x, 'tp', axis=2, tiled=True)  82.6 us
    all_to_all x1, blocking collectives, local(): lax.all_to_all(assembled.reshape(BUFFER, 1, feature_cols), 'seq', split_a...  10.6 us
    all_gather x1, blocking collectives, local(): key_part = lax.all_gather(keys, 'seq', axis=0, tiled=True)  9.25 us
    all_to_all x1, waiting for transfers between devices, local(): lax.all_to_all(outgoing, 'rep', split_axis=0, concat_axis=0, tiled=True)  9.09 us
    all_to_all x1, starting transfers between devices, local(): lax.all_to_all(outgoing, 'rep', split_axis=0, concat_axis=0, tiled=True)  9.08 us
  transfers between devices with their start and end apart: 4, of which 4 were waited for; matrix products, arithmetic and copies ran while one was open for 2% of the time, Pallas kernels for 0%

commit v1 on v0

--- a/solution.py
+++ b/solution.py
@@ -123,7 +123,8 @@
     query_weights = lax.all_gather(
         w_query.reshape(1, w_query.shape[0], w_query.shape[1]), "seq", axis=0, tiled=True
     )
-    feature_piece = lax.all_gather(local_x, "tp", axis=2, tiled=True)
+    copies = jnp.concatenate([local_x] * lax.axis_size("tp"), axis=2)
+    feature_piece = lax.all_to_all(copies, "tp", 2, 2, tiled=True)
     scaled_piece = (feature_piece.astype(jnp.float32) * gain_halves[None]).astype(jnp.bfloat16)
     query_acc = jnp.einsum(
         "rsn,snf->rf", scaled_piece, query_weights, preferred_element_type=jnp.float32

time: 441 us -> 313 us (0.71)
  waiting for transfers between devices: 365 us -> 181 us
  local copies, waits for them, and re-layouts: 8.3 us -> 50.9 us
  starting transfers between devices: 9.17 us -> 21.8 us
    all_gather x1, waiting for transfers between devices: 111 us -> 0.02 us  [local(): lax.all_gather(w_query.reshape(1, w_query.shape[0], w_query.shape[1]), 's...]
    all_to_all x0 -> x1, waiting for transfers between devices: none -> 103 us  [local(): feature_piece = lax.all_to_all(copies, 'tp', 2, 2, tiled=True)]
    psum x1, waiting for transfers between devices: 161 us -> 67.9 us  [local(): kv_total = lax.psum(kv_partial, 'tp')]
    all_gather x1 -> x0, waiting for transfers between devices: 82.6 us -> none  [local(): feature_piece = lax.all_gather(local_x, 'tp', axis=2, tiled=True)]
    unnamed x9 -> x40, local copies, waits for them, and re-layouts: 2.38 us -> 22.4 us
    all_to_all x0 -> x1, starting transfers between devices: none -> 12.6 us  [local(): feature_piece = lax.all_to_all(copies, 'tp', 2, 2, tiled=True)]
    concatenate x0 -> x2, local copies, waits for them, and re-layouts: none -> 11.6 us  [local(): copies = jnp.concatenate([local_x] * lax.axis_size('tp'), axis=2)]
    all_to_all x0 -> x1, local copies, waits for them, and re-layouts: none -> 11 us  [local(): feature_piece = lax.all_to_all(copies, 'tp', 2, 2, tiled=True)]
  transfers between devices with their start and end apart: 4 -> 4, of which waited for: 4 -> 3; matrix products, arithmetic and copies ran while one was open for 2% -> 6% of each run, Pallas kernels for 0% -> 0%
where the time goes in v1:
time: 313 us; the launch traced here: 312 us
  waiting for transfers between devices  181 us (58%)
  local copies, waits for them, and re-layouts  50.9 us (16%)
  blocking collectives  28.6 us (9%)
  starting transfers between devices  21.8 us (7%)
  between operations  15.1 us (5%)
  other arithmetic  9.02 us (3%)
  matrix products  6.42 us (2%)
    all_to_all x1, waiting for transfers between devices, local(): feature_piece = lax.all_to_all(copies, 'tp', 2, 2, tiled=True)  103 us
    psum x1, waiting for transfers between devices, local(): kv_total = lax.psum(kv_partial, 'tp')  67.9 us
    unnamed x40, local copies, waits for them, and re-layouts  22.4 us
    all_to_all x1, starting transfers between devices, local(): feature_piece = lax.all_to_all(copies, 'tp', 2, 2, tiled=True)  12.6 us
    concatenate x2, local copies, waits for them, and re-layouts, local(): copies = jnp.concatenate([local_x] * lax.axis_size('tp'), axis=2)  11.6 us
    all_to_all x1, local copies, waits for them, and re-layouts, local(): feature_piece = lax.all_to_all(copies, 'tp', 2, 2, tiled=True)  11 us
    all_to_all x1, blocking collectives, local(): lax.all_to_all(assembled.reshape(BUFFER, 1, feature_cols), 'seq', split_a...  10.6 us
    all_gather x1, blocking collectives, local(): key_part = lax.all_gather(keys, 'seq', axis=0, tiled=True)  9.25 us
  transfers between devices with their start and end apart: 4, of which 3 were waited for; matrix products, arithmetic and copies ran while one was open for 6% of the time, Pallas kernels for 0%

profile of v1, /device:TPU:16, one launch (start us, length us, event | category | flops | bytes accessed | tf_op | source)
XLA Modules:
  0.0 312.5 jit_solution(17121237374833972818)
XLA Ops:
  7.4 0.8 copy.39
  8.3 0.8 copy.38
  10.0 3.5 %gather_fusion = bf16[1536,128]{1,0:T(8,128)(2,1)S(1)} fusion(bf16[384,128]{1,0:T(8,128)(2,1)} %param.6, s32[2048]{0:T(1024)S(1)} %pad_clamp_fusion), kind=kCustom, calls=%fused_computation | custom fusion | bytes 792576 | tf_op jit(solution)/shard_map/jit(_take)/gather | solution.py:72
  13.5 1.3 select_select_fusion
  14.8 9.1 %all-to-all-start = ((bf16[8,192,128]{2,1,0:T(8,128)(2,1)}), bf16[8,192,128]{2,1,0:T(8,128)(2,1)S(1)}, u32[]{:S(2)}, u32[]{:S(2)}) async-start(bf16[8,192,128]{2,1,0:T(8,128)(2,1)} %select_select_fusion), calls=%async_computation | async-start | bytes 786432 | tf_op jit(solution)/shard_map/all_to_all | solution.py:107
  24.1 9.1 %all-to-all-done = bf16[8,192,128]{2,1,0:T(8,128)(2,1)S(1)} async-done(((bf16[8,192,128]{2,1,0:T(8,128)(2,1)}), bf16[8,192,128]{2,1,0:T(8,128)(2,1)S(1)}, u32[]{:S(2)}, u32[]{:S(2)}) %all-to-all-start) | async-done | bytes 393248 | tf_op jit(solution)/shard_map/all_to_all | solution.py:107
  33.2 1.4 gather_fusion.1
  36.0 10.6 %all_to_all.32 = bf16[2,2,12288]{2,1,0:T(2,128)(2,1)S(1)} all-to-all(bf16[2,2,12288]{2,1,0:T(2,128)(2,1)S(1)} %reshape.478), channel_id=1, replica_groups=mesh['rep'=8,'seq'=2,'tp'=32] {'seq'}, dimensions={0} | all-to-all | bytes 196608 | tf_op jit(solution)/shard_map/all_to_all | solution.py:112
  47.4 0.7 constant_dynamic-update-slice_fusion.30
  48.1 0.7 constant_dynamic-update-slice_fusion.29
  50.1 0.7 constant_dynamic-update-slice_fusion.26
  51.4 0.7 constant_dynamic-update-slice_fusion.24
  52.7 0.7 constant_dynamic-update-slice_fusion.22
  54.1 0.7 constant_dynamic-update-slice_fusion.20
  58.7 0.7 constant_dynamic-update-slice_fusion.13
  59.4 0.7 constant_dynamic-update-slice_fusion.12
  61.4 0.7 constant_dynamic-update-slice_fusion.9
  65.4 0.7 constant_dynamic-update-slice_fusion.3
  67.4 0.7 constant_dynamic-update-slice_fusion
  68.1 11.0 %copy.41 = bf16[192,2,4096]{0,1,2:T(2,128)(2,1)} copy(bf16[192,2,4096]{2,0,1:T(8,128)(2,1)} %constant_dynamic-update-slice_fusion) | data formatting | bytes 6291456 | tf_op jit(solution)/shard_map/concatenate | solution.py:126
  79.0 12.6 %all-to-all-start.2 = ((bf16[192,2,4096]{0,1,2:T(2,128)(2,1)}), bf16[192,2,4096]{0,1,2:T(2,128)(2,1)}, u32[]{:S(2)}, u32[]{:S(2)}) async-start(bf16[192,2,4096]{0,1,2:T(2,128)(2,1)} %copy.41), calls=%async_computation.2 | async-start | bytes 8388608 | tf_op jit(solution)/shard_map/all_to_all | solution.py:127
  91.7 0.7 all-gather.4.cloned.1.call-update
  92.8 1.5 convolution_bitcast_fusion
  94.8 102.9 %all-to-all-done.2 = bf16[192,2,4096]{0,1,2:T(2,128)(2,1)} async-done(((bf16[192,2,4096]{0,1,2:T(2,128)(2,1)}), bf16[192,2,4096]{0,1,2:T(2,128)(2,1)}, u32[]{:S(2)}, u32[]{:S(2)}) %all-to-all-start.2) | async-done | bytes 3145760 | tf_op jit(solution)/shard_map/all_to_all | solution.py:127
  197.7 11.0 %copy.42 = bf16[192,2,4096]{2,0,1:T(8,128)(2,1)} copy(bf16[192,2,4096]{0,1,2:T(2,128)(2,1)} %all-to-all-done.2) | data formatting | bytes 6291456 | tf_op jit(solution)/shard_map/all_to_all | solution.py:127
  208.7 2.6 fusion
  211.3 4.2 %fusion.6 = f32[24,2,8,128]{3,2,1,0:T(8,128)S(1)} fusion(bf16[2,4096,256]{2,1,0:T(8,128)(2,1)} %bitcast.71, bf16[192,2,4096]{2,0,1:T(8,128)(2,1)} %copy.42, f32[2,4096]{1,0:T(2,128)S(1)} %mul.228), kind=kOutput, calls=%fused_computation.12 | convolution fusion | flops 810024960 | bytes 7569408 | tf_op jit(solution)/shard_map/rsn,snf->rf/dot_general | solution.py:129
  215.6 67.9 %all-reduce.2.cloned.1.call-done = f32[192,2048]{1,0:T(8,128)} async-done(((f32[192,2048]{1,0:T(8,128)}), f32[192,2048]{1,0:T(8,128)}) %all-reduce.2.cloned.1.call-update) | async-done | bytes 1572880 | tf_op jit(solution)/shard_map/psum | solution.py:141
  283.5 1.0 fusion.27
  285.1 9.2 %all-gather.1 = bf16[384,1,128]{2,0,1:T(8,128)(2,1)S(1)} all-gather(bf16[192,1,128]{2,0,1:T(8,128)(2,1)S(1)} %pad_maximum_fusion), channel_id=3, replica_groups=mesh['rep'=8,'seq'=2,'tp'=32] {'seq'}, dimensions={0}, use_global_device_ids=true | all-gather | bytes 147456 | tf_op jit(solution)/shard_map/all_gather | solution.py:149
  294.9 8.8 %all_gather.11 = bf16[384,128]{1,0:T(8,128)(2,1)S(1)} all-gather(bf16[192,128]{1,0:T(8,128)(2,1)S(1)} %get-tuple-element.19), channel_id=1, replica_groups=mesh['rep'=8,'seq'=2,'tp'=32] {'seq'}, dimensions={0}, use_global_device_ids=true | all-gather | bytes 147456 | tf_op jit(solution)/shard_map/all_gather | solution.py:150
  304.3 0.7 bitcast_select_fusion
  (74 shorter events, 19.2 us)
Async XLA Ops:
  7.4 85.5 %copy-start = (bf16[2,128,2048]{2,1,0:T(8,128)(2,1)S(1)}, bf16[2,128,2048]{2,1,0:T(8,128)(2,1)}, u32[]{:S(2)}) copy-start(bf16[2,128,2048]{2,1,0:T(8,128)(2,1)} %param.9) | copy-start | bytes 3145732
  14.8 18.4 %all-to-all-start = ((bf16[8,192,128]{2,1,0:T(8,128)(2,1)}), bf16[8,192,128]{2,1,0:T(8,128)(2,1)S(1)}, u32[]{:S(2)}, u32[]{:S(2)}) async-start(bf16[8,192,128]{2,1,0:T(8,128)(2,1)} %select_select_fusion), calls=%async_computation | async-start | bytes 786432 | tf_op jit(solution)/shard_map/all_to_all | solution.py:107
  79.0 13.4 %copy-start.1 = (f32[8192]{0:T(1024)S(1)}, f32[8192]{0:T(1024)}, u32[]{:S(2)}) copy-start(f32[8192]{0:T(1024)} %param.7) | copy-start | bytes 98308
  79.0 118.7 %all-to-all-start.2 = ((bf16[192,2,4096]{0,1,2:T(2,128)(2,1)}), bf16[192,2,4096]{0,1,2:T(2,128)(2,1)}, u32[]{:S(2)}, u32[]{:S(2)}) async-start(bf16[192,2,4096]{0,1,2:T(2,128)(2,1)} %copy.41), calls=%async_computation.2 | async-start | bytes 8388608 | tf_op jit(solution)/shard_map/all_to_all | solution.py:127
  91.6 119.7 %all-gather.4.cloned.1.call-start = ((), (), s32[]{:S(2)}) async-start(), calls=%async_computation.4 | async-start | bytes 6291456 | tf_op jit(solution)/shard_map/all_gather | solution.py:123
  92.4 191.1 %all-reduce.2.cloned.1.call-start = ((), (), s32[]{:S(2)}) async-start(), calls=%async_computation.3 | async-start | bytes 3145728 | tf_op jit(solution)/shard_map/psum | solution.py:141
Sparse Core Ops, SparseCore 0:
  94.8 111.0 all-gather.3
Sparse Core Ops, SparseCore 1:
  96.2 187.2 all-reduce.1
